TPU v7x, 32 devices: a whole 2x2x4 slice. The times are simulated.
32 devices in a mesh: dp: 4 (over z), expert: 8 (over y, x, core).
Axes of the slice: x: 2, y: 2, z: 4, core: 2. Of those that a mesh axis runs over, the one named last changes fastest.
Arguments:
- hidden: bfloat16 [3072, 2880], P('expert', 'dp'), may hold values from -6 to 6
- segments: int32 [8, 384], P('expert'), may hold values from 0 to 3, never falling along the last dimension, each value on 1 to 192 neighbouring positions
- request_adapter: int32 [8, 4], P('expert'), may hold values from 0 to 7
- routes: int32 [8, 384, 4], P('expert', 'dp'), may hold values from 0 to 7, all different within a row; in each aligned block of 96 rows (0 to 95, 96 to 191, ..., all dimensions but the last counted through in order) at most 64 rows name the same one
- expert_gates: bfloat16 [8, 384, 4], P('expert', 'dp'), may hold values from 0.049804688 to 0.59765625
- attention_gain: float32 [2880], replicated, may hold values from 0.25 to 1.75
- joined_weight: bfloat16 [2880, 4, 640], P(None, 'dp'), may hold values from -0.109375 to 0.109375
- sinks: float32 [32], P('dp'), may hold values from 0 to 3
- attention_out_weight: bfloat16 [2048, 2880], P('dp'), may hold values from -0.125 to 0.125
- joined_down_maps: bfloat16 [2880, 128], replicated, may hold values from -0.109375 to 0.109375
- joined_up_maps: bfloat16 [128, 4, 640], P(None, 'dp'), may hold values from -0.375 to 0.375
- output_down_maps: bfloat16 [2048, 128], P('dp'), may hold values from -0.125 to 0.125
- output_up_maps: bfloat16 [128, 2880], P(None, 'dp'), may hold values from -0.75 to 0.75
- expert_norm_gain: float32 [2880], replicated, may hold values from 0.25 to 1.75
- expert_gate_weight: bfloat16 [8, 2880, 2880], P('expert', None, 'dp'), may hold values from -0.109375 to 0.109375
- expert_up_weight: bfloat16 [8, 2880, 2880], P('expert', None, 'dp'), may hold values from -0.109375 to 0.109375
- expert_down_weight: bfloat16 [8, 2880, 2880], P('expert', 'dp'), may hold values from -0.109375 to 0.109375
- closing_gain: float32 [2880], replicated, may hold values from 0.25 to 1.75
- vocabulary_weight: bfloat16 [2880, 25600], P(None, ('dp', 'expert')), may hold values from -0.109375 to 0.109375
Outputs:
- hidden_out: bfloat16 [3072, 2880], P('expert', 'dp')
- logits: float32 [32, 25600], P(None, ('dp', 'expert'))
Inputs may be any that keep to these rules, and one draw needn't show every extreme that they name: `segments`: in each column the ids do not fall; each of the 4 requests has 1 to 192 tokens, and one has exactly 192. `routes`: the 4 experts of a token differ. Within the rows of one device (96 consecutive tokens, aligned blocks) no expert is named more than 64 times, and in some blocks one expert is named exactly 64 times.
All inputs are finite; a program needn't handle non-finite values.
Results may differ from a plain program's by a relative error of at most 0.02.
Values may be sent and summed in bfloat16 or wider, within the bound.
No kernel may reach another device: no remote copies, remote signals or barrier semaphores. Data moves between devices by JAX's collectives and lax.ppermute only.
A program may use at most 128 MiB of HBM per device.

v0:
```python
import jax
import jax.numpy as jnp
from jax import lax
from jax.sharding import PartitionSpec as P

HEAD_SIZE = 64
QUERY_GROUP = 8
TOP = 4
ADAPTER_RANK = 16
REQS = 4
epsilon = 1e-05
theta_base = 150000.0
adapter_scale = 2.0
glu_alpha = 1.702


def rms_scale(values, gain_row):
    mean_square = jnp.mean(values * values, axis=-1, keepdims=True)
    return values * lax.rsqrt(mean_square + epsilon) * gain_row


def positions_of(segment_row):
    counter = jnp.arange(segment_row.shape[0], dtype=jnp.int32)
    starting = jnp.concatenate(
        [jnp.ones((1,), dtype=jnp.bool_), segment_row[1:] != segment_row[:-1]]
    )
    first_index = lax.cummax(jnp.where(starting, counter, 0), axis=0)
    return counter - first_index


def adapter_per_token(segment_row, adapter_row):
    hits = segment_row[:, None] == jnp.arange(adapter_row.shape[0], dtype=jnp.int32)[None, :]
    return jnp.sum(jnp.where(hits, adapter_row[None, :], 0), axis=1)


def rotate_heads(values, positions):
    head_dim = values.shape[-1]
    half_dim = head_dim // 2
    frequency = theta_base ** (-2.0 * jnp.arange(half_dim, dtype=jnp.float32) / head_dim)
    angles = positions.astype(jnp.float32)[:, None] * frequency[None, :]
    cosine = jnp.cos(angles)[:, None, :]
    sine_part = jnp.sin(angles)[:, None, :]
    first_half = values[..., :half_dim]
    second_half = values[..., half_dim:]
    return jnp.concatenate(
        [
            first_half * cosine - second_half * sine_part,
            second_half * cosine + first_half * sine_part,
        ],
        axis=-1,
    )


def attend_heads(queries, key_heads, value_heads, segment_row, sink_row):
    tokens_now, kv_now, group_now, head_dim = queries.shape
    scores = jnp.einsum(
        "tkgh,skh->kgts", queries, key_heads, preferred_element_type=jnp.float32
    ) * head_dim ** (-0.5)
    counter = jnp.arange(tokens_now, dtype=jnp.int32)
    allowed = (segment_row[:, None] == segment_row[None, :]) & (
        counter[None, :] <= counter[:, None]
    )
    weights = jnp.where(allowed[None, None], jnp.exp(scores), 0.0)
    totals = jnp.sum(weights, axis=-1, keepdims=True) + jnp.exp(sink_row).reshape(
        kv_now, group_now, 1, 1
    )
    probs = (weights / totals).astype(jnp.bfloat16)
    blended_hidden = jnp.einsum(
        "kgts,skh->tkgh", probs, value_heads, preferred_element_type=jnp.float32
    )
    return blended_hidden.astype(jnp.bfloat16).reshape(tokens_now, kv_now * group_now * head_dim)


def shards(
    hidden,
    segments,
    request_adapter,
    routes,
    expert_gates,
    attention_gain,
    joined_weight,
    sinks,
    attention_out_weight,
    joined_down_maps,
    joined_up_maps,
    output_down_maps,
    output_up_maps,
    expert_norm_gain,
    expert_gate_weight,
    expert_up_weight,
    expert_down_weight,
    closing_gain,
    vocabulary_weight,
):
    groups = lax.axis_size("dp")
    columns = lax.axis_size("expert")
    position_dp = lax.axis_index("dp")
    segment_row = segments[0]
    adapter_row = request_adapter[0]
    col_tokens = segment_row.shape[0]
    gathered_rows = lax.all_gather(hidden, "dp", axis=1, tiled=True)
    width = gathered_rows.shape[1]
    normalized_hidden = rms_scale(gathered_rows.astype(jnp.float32), attention_gain).astype(
        jnp.bfloat16
    )
    joined_projection = jnp.dot(
        normalized_hidden, joined_weight.reshape(width, -1), preferred_element_type=jnp.float32
    )
    reduced_every_adapter = joined_down_maps.shape[1]
    reduced_hidden = jnp.dot(
        normalized_hidden, joined_down_maps, preferred_element_type=jnp.float32
    ).astype(jnp.bfloat16)
    rank_owner = jnp.arange(reduced_every_adapter, dtype=jnp.int32) // ADAPTER_RANK
    adapter_mask = adapter_per_token(segment_row, adapter_row)[:, None] == rank_owner[None, :]
    selected_reduced = jnp.where(adapter_mask, reduced_hidden, jnp.zeros_like(reduced_hidden))
    joined_projection = joined_projection + adapter_scale * jnp.dot(
        selected_reduced,
        joined_up_maps.reshape(reduced_every_adapter, -1),
        preferred_element_type=jnp.float32,
    )
    kv_here = joined_weight.shape[1]
    joined_projection = joined_projection.reshape(col_tokens, kv_here, QUERY_GROUP + 2, HEAD_SIZE)
    positions = positions_of(segment_row)
    queries = rotate_heads(
        joined_projection[:, :, :QUERY_GROUP].reshape(col_tokens, kv_here * QUERY_GROUP, HEAD_SIZE),
        positions,
    )
    queries = queries.astype(jnp.bfloat16).reshape(col_tokens, kv_here, QUERY_GROUP, HEAD_SIZE)
    key_heads = rotate_heads(joined_projection[:, :, QUERY_GROUP], positions).astype(jnp.bfloat16)
    value_heads = joined_projection[:, :, QUERY_GROUP + 1].astype(jnp.bfloat16)
    blended_hidden = attend_heads(queries, key_heads, value_heads, segment_row, sinks)
    partial_out = jnp.dot(blended_hidden, attention_out_weight, preferred_element_type=jnp.float32)
    mine_out = lax.psum_scatter(
        partial_out.astype(jnp.bfloat16), "dp", scatter_dimension=1, tiled=True
    ).astype(jnp.float32)
    output_reduced = lax.psum(
        jnp.dot(blended_hidden, output_down_maps, preferred_element_type=jnp.float32).astype(
            jnp.bfloat16
        ),
        "dp",
    )
    selected_output = jnp.where(adapter_mask, output_reduced, jnp.zeros_like(output_reduced))
    adapter_delta = adapter_scale * jnp.dot(
        selected_output, output_up_maps, preferred_element_type=jnp.float32
    )
    resid = (hidden.astype(jnp.float32) + mine_out + adapter_delta).astype(jnp.bfloat16)
    share = col_tokens // groups
    column_full = lax.all_gather(resid, "dp", axis=1, tiled=True)
    own_rows = lax.dynamic_slice_in_dim(column_full, position_dp * share, share, 0)
    moe_in = rms_scale(
        lax.optimization_barrier(own_rows).astype(jnp.float32), expert_norm_gain
    ).astype(jnp.bfloat16)
    experts = expert_gate_weight.shape[0] * columns
    capacity = 4 * share * TOP // (3 * experts)
    route_flat = routes[0].reshape(-1)
    one_hot = (route_flat[:, None] == jnp.arange(experts, dtype=jnp.int32)[None, :]).astype(
        jnp.int32
    )
    slot_rows = jnp.sum((jnp.cumsum(one_hot, axis=0) - one_hot) * one_hot, axis=1)
    target = route_flat * capacity + slot_rows
    source_rows = jnp.arange(route_flat.shape[0], dtype=jnp.int32) // TOP
    table = jnp.full((experts * capacity,), share, jnp.int32).at[target].set(source_rows)
    padded = jnp.concatenate([moe_in, jnp.zeros((1, width), jnp.bfloat16)], axis=0)
    outgoing = jnp.take(padded, table, axis=0).reshape(experts, capacity, width)
    gate_weight = expert_gate_weight[0]
    up_weight = expert_up_weight[0]
    down_weight = expert_down_weight[0]
    copies = jnp.tile(outgoing, (groups, 1, 1))
    arrived = lax.all_to_all(copies, ("dp", "expert"), split_axis=0, concat_axis=0, tiled=True)
    senders = arrived.shape[0]
    slots_now = arrived.shape[1]
    rows_in = arrived.reshape(-1, width)
    gate_part = jnp.dot(rows_in, gate_weight, preferred_element_type=jnp.float32)
    up_part = jnp.dot(rows_in, up_weight, preferred_element_type=jnp.float32)
    activated = (gate_part * jax.nn.sigmoid(glu_alpha * gate_part) * (up_part + 1.0)).astype(
        jnp.bfloat16
    )
    shares_out = (
        jnp.dot(activated, down_weight, preferred_element_type=jnp.float32)
        .astype(jnp.bfloat16)
        .reshape(senders, slots_now, width)
    )
    answers = lax.all_to_all(shares_out, ("dp", "expert"), split_axis=0, concat_axis=0, tiled=True)
    merged = jnp.sum(
        answers.reshape(groups, columns, capacity, width).astype(jnp.float32), axis=0
    ).astype(jnp.bfloat16)
    picked_out = jnp.take(merged.reshape(experts * capacity, width), target, axis=0).reshape(
        share, TOP, width
    )
    mixture = jnp.einsum(
        "tk,tkd->td", expert_gates[0], picked_out, preferred_element_type=jnp.float32
    )
    moe_rounded = lax.optimization_barrier(mixture.astype(jnp.bfloat16))
    finished = (own_rows.astype(jnp.float32) + moe_rounded.astype(jnp.float32)).astype(jnp.bfloat16)
    hidden_out = lax.all_to_all(finished, "dp", split_axis=1, concat_axis=0, tiled=True)
    counter = jnp.arange(col_tokens, dtype=jnp.int32)
    request_ids = jnp.arange(REQS, dtype=jnp.int32)
    last_index = jnp.max(
        jnp.where(segment_row[None, :] == request_ids[:, None], counter[None, :], -1), axis=1
    )
    local_index = last_index - position_dp * share
    inside = (local_index >= 0) & (local_index < share)
    chosen = jnp.take(finished, jnp.clip(local_index, 0, share - 1), axis=0)
    chosen = jnp.where(inside[:, None], chosen, jnp.zeros_like(chosen))
    ends = rms_scale(chosen.astype(jnp.float32), closing_gain).astype(jnp.bfloat16)
    spread_rows = lax.all_gather(ends, ("dp", "expert"), axis=0, tiled=True)
    tail_rows = jnp.sum(
        spread_rows.reshape(groups, columns * REQS, width).astype(jnp.float32), axis=0
    ).astype(jnp.bfloat16)
    logits = jnp.dot(tail_rows, vocabulary_weight, preferred_element_type=jnp.float32)
    return (hidden_out, logits)


def solution(mesh):
    in_specs = (
        P("expert", "dp"),
        P("expert", None),
        P("expert", None),
        P("expert", "dp", None),
        P("expert", "dp", None),
        P(),
        P(None, "dp", None),
        P("dp"),
        P("dp", None),
        P(),
        P(None, "dp", None),
        P("dp", None),
        P(None, "dp"),
        P(),
        P("expert", None, "dp"),
        P("expert", None, "dp"),
        P("expert", "dp", None),
        P(),
        P(None, ("dp", "expert")),
    )
    out_specs = (P("expert", "dp"), P(None, ("dp", "expert")))
    return jax.shard_map(shards, mesh=mesh, in_specs=in_specs, out_specs=out_specs, check_vma=False)
```

profile of v0, /device:TPU:0, one launch (start us, length us, event | category | flops | bytes accessed | tf_op | source)
XLA Modules:
  0.0 916.7 jit_solution(5084641404369946867)
XLA Ops:
  7.2 0.7 all-gather.4.cloned.1.call-update
  8.0 0.8 reduce.4
  8.8 0.8 compare_reduce_fusion
  10.1 0.7 exp.18
  10.9 0.7 select_reduce_fusion.1
  12.1 48.3 %all-gather.4.cloned.1.call-done = bf16[384,2880]{0,1:T(8,128)(2,1)} async-done(((bf16[384,720]{0,1:T(8,128)(2,1)}), bf16[384,2880]{0,1:T(8,128)(2,1)}) %all-gather.4.cloned.1.call-update) | async-done | bytes 2211856 | tf_op jit(solution)/shard_map/all_gather | solution.py:101
  60.4 2.2 fusion
  62.6 5.9 fusion.11
  68.5 4.8 fusion.21
  73.3 2.5 copy.59
  75.8 1.2 slice_bitcast_fusion
  77.0 0.9 slice_bitcast_fusion.1
  78.3 1.3 fusion.10
  79.6 2.2 fusion.23
  81.9 0.7 copy-done.3
  82.6 1.0 convolution_convert_fusion.2
  83.7 4.1 convolution_convert_fusion.1
  87.9 29.0 %all-reduce.3.cloned.1.call-done = bf16[384,128]{1,0:T(8,128)(2,1)} async-done(((bf16[384,128]{1,0:T(8,128)(2,1)}), bf16[384,128]{1,0:T(8,128)(2,1)}) %all-reduce.3.cloned.1.call-update) | async-done | bytes 98320 | tf_op jit(solution)/shard_map/psum | solution.py:136
  116.8 48.0 %reduce-scatter.2.cloned.1.call-done = bf16[384,720]{0,1:T(8,128)(2,1)} async-done(((bf16[384,2880]{0,1:T(8,128)(2,1)}), bf16[384,720]{0,1:T(8,128)(2,1)}) %reduce-scatter.2.cloned.1.call-update) | async-done | bytes 552976 | tf_op jit(solution)/shard_map/reduce_scatter | solution.py:133
  164.9 2.4 fusion.22
  167.7 0.9 reduce-window.19
  169.2 3.1 scatter_custom_fusion
  172.4 42.6 %all-gather.6.cloned.1.call-done = bf16[384,2880]{0,1:T(8,128)(2,1)} async-done(((bf16[384,720]{0,1:T(8,128)(2,1)}), bf16[384,2880]{0,1:T(8,128)(2,1)}) %all-gather.6.cloned.1.call-update) | async-done | bytes 2211856 | tf_op jit(solution)/shard_map/all_gather | solution.py:148
  215.0 1.7 constant_dynamic-slice_fusion
  216.7 0.4 fusion.17
  217.1 0.4 fusion.19
  217.9 3.7 gather_fusion
  221.6 2.2 broadcast_select_fusion
  223.8 6.0 tile.8
  229.8 266.5 %all_to_all.29 = bf16[32,64,2880]{2,1,0:T(8,128)(2,1)} all-to-all(bf16[32,64,2880]{2,1,0:T(8,128)(2,1)} %bitcast.115), channel_id=1, replica_groups=mesh['dp'=4,'expert'=8] {'dp','expert'}, dimensions={0} | all-to-all | bytes 23592960 | tf_op jit(solution)/shard_map/all_to_all | solution.py:169
  496.3 15.1 %fusion.4 = f32[2048,720]{0,1:T(8,128)} fusion(bf16[2048,2880]{1,0:T(8,128)(2,1)} %bitcast.26, bf16[1,2880,720]{1,2,0:T(8,128)(2,1)} %param.34), kind=kOutput, calls=%fused_computation.15 | convolution fusion | flops 8493465600 | bytes 21841920 | tf_op jit(solution)/shard_map/dot_general | solution.py:174
  511.4 26.6 %convolution_convert_fusion = bf16[2048,2880]{0,1:T(8,128)(2,1)} fusion(bf16[1,720,2880]{2,1,0:T(8,128)(2,1)} %param.35, f32[2048,720]{0,1:T(8,128)} %fusion.4, bf16[2048,2880]{1,0:T(8,128)(2,1)} %bitcast.26, bf16[1,2880,720]{1,2,0:T(8,128)(2,1)} %param.33), kind=kOutput, calls=%fused_computation.4 | convolution fusion | flops 17004625920 | bytes 37785600 | tf_op jit(solution)/shard_map/dot_general | solution.py:179
  538.0 16.3 %copy.67 = bf16[2048,2880]{1,0:T(8,128)(2,1)} copy(bf16[2048,2880]{0,1:T(8,128)(2,1)} %convolution_convert_fusion) | data formatting | bytes 23592960 | tf_op jit(solution)/shard_map/convert_element_type | solution.py:180
  554.4 4.1 all-to-all-start.1
  559.1 266.6 %all-to-all-done.1 = bf16[32,64,2880]{2,1,0:T(8,128)(2,1)} async-done(((bf16[32,64,2880]{2,1,0:T(8,128)(2,1)}), bf16[32,64,2880]{2,1,0:T(8,128)(2,1)}, u32[]{:S(2)}, u32[]{:S(2)}) %all-to-all-start.1) | async-done | bytes 11796512 | tf_op jit(solution)/shard_map/all_to_all | solution.py:183
  825.7 6.8 reduce_sum.89
  832.5 3.5 gather_fusion.1
  836.0 2.6 gather.19
  838.6 4.7 multiply_reduce_fusion
  843.6 1.7 add_convert_fusion
  845.7 0.6 gather_fusion.2
  846.5 1.1 copy.68
  847.6 3.5 all-to-all-start.2
  851.2 49.2 %all-gather = bf16[32,4,2880]{2,1,0:T(4,128)(2,1)} all-gather(bf16[1,4,2880]{2,1,0:T(4,128)(2,1)S(1)} %fusion.60), channel_id=1, replica_groups=mesh['dp'=4,'expert'=8] {'dp','expert'}, dimensions={0}, use_global_device_ids=true | all-gather | bytes 760320 | tf_op jit(solution)/shard_map/all_gather | solution.py:206
  900.4 2.3 reshape.444
  902.7 2.0 reduce_sum.91
  904.6 4.5 fusion.79
  909.1 1.0 copy.70
  (78 shorter events, 4.8 us)
Async XLA Ops:
  7.2 76.5 %copy-start = (bf16[512,2880]{0,1:T(8,128)(2,1)S(1)}, bf16[512,2880]{0,1:T(8,128)(2,1)}, u32[]{:S(2)}) copy-start(bf16[512,2880]{0,1:T(8,128)(2,1)} %param.27) | copy-start | bytes 8847364
  7.2 53.2 %all-gather.4.cloned.1.call-start = ((), (), s32[]{:S(2)}) async-start(), calls=%async_computation.4 | async-start | bytes 2764800 | tf_op jit(solution)/shard_map/all_gather | solution.py:101
  7.9 108.9 %all-reduce.3.cloned.1.call-start = ((), (), s32[]{:S(2)}) async-start(), calls=%async_computation.6 | async-start | bytes 196608 | tf_op jit(solution)/shard_map/psum | solution.py:136
  62.6 6.0 copy-start.9
  62.6 6.0 copy-start.10
  79.6 3.0 copy-start.4
  81.9 0.8 copy-start.3
  83.6 81.3 %copy-start.2 = (bf16[384,720]{0,1:T(8,128)(2,1)S(1)}, bf16[384,720]{0,1:T(8,128)(2,1)}, u32[]{:S(2)}) copy-start(bf16[384,720]{0,1:T(8,128)(2,1)} %param.19) | copy-start | bytes 1658884
  83.6 81.3 %reduce-scatter.2.cloned.1.call-start = ((), (), s32[]{:S(2)}) async-start(), calls=%async_computation.5 | async-start | bytes 2764800 | tf_op jit(solution)/shard_map/reduce_scatter | solution.py:133
  87.8 79.6 %copy-start.5 = (s32[1,96,4]{1,2,0:T(4,128)S(1)}, s32[1,96,4]{1,2,0:T(4,128)}, u32[]{:S(2)}) copy-start(s32[1,96,4]{1,2,0:T(4,128)} %param.22) | copy-start | bytes 4612
  87.8 129.3 %copy-start.6 = (f32[2880]{0:T(1024)S(1)}, f32[2880]{0:T(1024)}, u32[]{:S(2)}) copy-start(f32[2880]{0:T(1024)} %param.32) | copy-start | bytes 34564
  87.8 127.2 %all-gather.6.cloned.1.call-start = ((), (), s32[]{:S(2)}) async-start(), calls=%async_computation.7 | async-start | bytes 2764800 | tf_op jit(solution)/shard_map/all_gather | solution.py:148
  554.4 4.4 copy-start.8
  554.4 271.3 %all-to-all-start.1 = ((bf16[32,64,2880]{2,1,0:T(8,128)(2,1)}), bf16[32,64,2880]{2,1,0:T(8,128)(2,1)}, u32[]{:S(2)}, u32[]{:S(2)}) async-start(bf16[32,64,2880]{2,1,0:T(8,128)(2,1)} %bitcast.114), calls=%async_computation.2 | async-start | bytes 24117248 | tf_op jit(solution)/shard_map/all_to_all | solution.py:183
  843.2 7.8 copy-start.7
  847.6 61.5 %all-to-all-start.2 = ((bf16[96,4,720]{2,0,1:T(8,128)(2,1)}), bf16[96,4,720]{2,0,1:T(8,128)(2,1)S(1)}, u32[]{:S(2)}, u32[]{:S(2)}) async-start(bf16[96,4,720]{2,0,1:T(8,128)(2,1)} %copy.68), calls=%async_computation.3 | async-start | bytes 1179648 | tf_op jit(solution)/shard_map/all_to_all | solution.py:195
  851.2 59.0 %copy-start.1 = (bf16[512,2880]{0,1:T(8,128)(2,1)S(1)}, bf16[512,2880]{0,1:T(8,128)(2,1)}, u32[]{:S(2)}) copy-start(bf16[512,2880]{0,1:T(8,128)(2,1)} %param.27) | copy-start | bytes 8847364
Sparse Core Ops, SparseCore 0:
  9.6 50.7 all-gather.3
  83.7 33.0 all-reduce.2
  119.3 45.5 reduce-scatter.1
  167.5 47.4 all-gather.5
where the time goes:
time: 918 us; the launch traced here: 917 us
  waiting for transfers between devices  435 us (47%)
  blocking collectives  316 us (34%)
  matrix products  68 us (7%)
  local copies, waits for them, and re-layouts  50.3 us (5%)
  other arithmetic  25.7 us (3%)
  between operations  14.1 us (2%)
    all_to_all x1, waiting for transfers between devices, shards(): lax.all_to_all(shares_out, ('dp', 'expert'), split_axis=0, concat_axis=0,...  267 us
    all_to_all x1, blocking collectives, shards(): lax.all_to_all(copies, ('dp', 'expert'), split_axis=0, concat_axis=0, til...  266 us
    all_gather x1, blocking collectives, shards(): spread_rows = lax.all_gather(ends, ('dp', 'expert'), axis=0, tiled=True)  49.2 us
    all_gather x1, waiting for transfers between devices, shards(): gathered_rows = lax.all_gather(hidden, 'dp', axis=1, tiled=True)  48.3 us
    reduce_scatter x1, waiting for transfers between devices, shards(): lax.psum_scatter(partial_out.astype(jnp.bfloat16), 'dp', scatter_dimensio...  48 us
    all_gather x1, waiting for transfers between devices, shards(): column_full = lax.all_gather(resid, 'dp', axis=1, tiled=True)  42.6 us
    psum x1, waiting for transfers between devices, shards(): lax.psum(jnp.dot(blended_hidden, output_down_maps, preferred_element_type...  29 us
    dot_general x1, matrix products, shards(): jnp.dot(activated, down_weight, preferred_element_type=jnp.float32)  26.6 us
  transfers between devices with their start and end apart: 6, of which 5 were waited for; matrix products, arithmetic and copies ran while one was open for 2% of the time, Pallas kernels for 0%

commit v1 on v0

--- a/solution.py
+++ b/solution.py
@@ -133,11 +133,14 @@
     mine_out = lax.psum_scatter(
         partial_out.astype(jnp.bfloat16), "dp", scatter_dimension=1, tiled=True
     ).astype(jnp.float32)
-    output_reduced = lax.psum(
-        jnp.dot(blended_hidden, output_down_maps, preferred_element_type=jnp.float32).astype(
-            jnp.bfloat16
+    output_reduced = jnp.sum(
+        lax.all_gather(
+            jnp.dot(blended_hidden, output_down_maps, preferred_element_type=jnp.float32).astype(
+                jnp.bfloat16
+            ),
+            "dp",
         ),
-        "dp",
+        axis=0,
     )
     selected_output = jnp.where(adapter_mask, output_reduced, jnp.zeros_like(output_reduced))
     adapter_delta = adapter_scale * jnp.dot(

time: 918 us -> 888 us (0.967)
  waiting for transfers between devices: 435 us -> 389 us
  blocking collectives: 316 us -> 333 us
    psum x1 -> x0, waiting for transfers between devices: 29 us -> none  [shards(): lax.psum(jnp.dot(blended_hidden, output_down_maps, preferred_element_type...]
    reduce_scatter x1, waiting for transfers between devices: 48 us -> 29.5 us  [shards(): lax.psum_scatter(partial_out.astype(jnp.bfloat16), 'dp', scatter_dimensio...]
    all_gather x0 -> x1, blocking collectives: none -> 17.8 us  [shards(): lax.all_gather(jnp.dot(blended_hidden, output_down_maps, preferred_elemen...]
  transfers between devices with their start and end apart: 6 -> 5, of which waited for: 5 -> 4; matrix products, arithmetic and copies ran while one was open for 2% -> 2% of each run, Pallas kernels for 0% -> 0%
where the time goes in v1:
time: 888 us; the launch traced here: 887 us
  waiting for transfers between devices  389 us (44%)
  blocking collectives  333 us (38%)
  matrix products  67.3 us (8%)
  local copies, waits for them, and re-layouts  50.2 us (6%)
  other arithmetic  25.7 us (3%)
  between operations  14.1 us (2%)
    all_to_all x1, waiting for transfers between devices, shards(): lax.all_to_all(shares_out, ('dp', 'expert'), split_axis=0, concat_axis=0,...  267 us
    all_to_all x1, blocking collectives, shards(): lax.all_to_all(copies, ('dp', 'expert'), split_axis=0, concat_axis=0, til...  266 us
    all_gather x1, blocking collectives, shards(): spread_rows = lax.all_gather(ends, ('dp', 'expert'), axis=0, tiled=True)  49.2 us
    all_gather x1, waiting for transfers between devices, shards(): gathered_rows = lax.all_gather(hidden, 'dp', axis=1, tiled=True)  48.3 us
    all_gather x1, waiting for transfers between devices, shards(): column_full = lax.all_gather(resid, 'dp', axis=1, tiled=True)  43.5 us
    reduce_scatter x1, waiting for transfers between devices, shards(): lax.psum_scatter(partial_out.astype(jnp.bfloat16), 'dp', scatter_dimensio...  29.5 us
    dot_general x1, matrix products, shards(): jnp.dot(activated, down_weight, preferred_element_type=jnp.float32)  26.6 us
    all_gather x1, blocking collectives, shards(): lax.all_gather(jnp.dot(blended_hidden, output_down_maps, preferred_elemen...  17.8 us
  transfers between devices with their start and end apart: 5, of which 4 were waited for; matrix products, arithmetic and copies ran while one was open for 2% of the time, Pallas kernels for 0%

profile of v1, /device:TPU:0, one launch (start us, length us, event | category | flops | bytes accessed | tf_op | source)
XLA Modules:
  0.0 887.0 jit_solution(6553532632163200640)
XLA Ops:
  7.2 0.7 all-gather.5.cloned.1.call-update
  8.0 0.8 reduce.5
  8.8 0.8 compare_reduce_fusion
  10.1 0.7 exp.18
  10.9 0.7 select_reduce_fusion.1
  12.1 48.3 %all-gather.5.cloned.1.call-done = bf16[384,2880]{0,1:T(8,128)(2,1)} async-done(((bf16[384,720]{0,1:T(8,128)(2,1)}), bf16[384,2880]{0,1:T(8,128)(2,1)}) %all-gather.5.cloned.1.call-update) | async-done | bytes 2211856 | tf_op jit(solution)/shard_map/all_gather | solution.py:101
  60.4 2.2 fusion
  62.6 5.9 fusion.11
  68.5 4.8 fusion.21
  73.3 2.5 copy.59
  75.8 1.2 slice_bitcast_fusion
  77.0 0.9 slice_bitcast_fusion.1
  78.3 1.3 fusion.10
  79.6 2.2 fusion.23
  81.9 0.7 copy-done.3
  82.6 3.1 convolution_convert_fusion.1
  85.8 1.3 convolution_convert_fusion.2
  87.1 17.8 %all-gather = bf16[1536,128]{1,0:T(8,128)(2,1)S(1)} all-gather(bf16[384,128]{1,0:T(8,128)(2,1)S(1)} %convolution_convert_fusion.2), channel_id=2, replica_groups=mesh['dp'=4,'expert'=8] {'dp'}, dimensions={0}, use_global_device_ids=true | all-gather | bytes 491520 | tf_op jit(solution)/shard_map/all_gather | solution.py:137
  105.0 29.5 %reduce-scatter.2.cloned.1.call-done = bf16[384,720]{0,1:T(8,128)(2,1)} async-done(((bf16[384,2880]{0,1:T(8,128)(2,1)}), bf16[384,720]{0,1:T(8,128)(2,1)}) %reduce-scatter.2.cloned.1.call-update) | async-done | bytes 552976 | tf_op jit(solution)/shard_map/reduce_scatter | solution.py:133
  134.5 2.4 fusion.22
  137.3 0.9 reduce-window.19
  138.8 2.9 scatter_custom_fusion
  141.8 43.5 %all-gather.7.cloned.1.call-done = bf16[384,2880]{0,1:T(8,128)(2,1)} async-done(((bf16[384,720]{0,1:T(8,128)(2,1)}), bf16[384,2880]{0,1:T(8,128)(2,1)}) %all-gather.7.cloned.1.call-update) | async-done | bytes 2211856 | tf_op jit(solution)/shard_map/all_gather | solution.py:151
  185.3 1.7 constant_dynamic-slice_fusion
  186.9 0.4 fusion.17
  187.4 0.4 fusion.19
  188.2 3.7 gather_fusion
  191.9 2.2 broadcast_select_fusion
  194.1 6.0 tile.8
  200.1 266.5 %all_to_all.29 = bf16[32,64,2880]{2,1,0:T(8,128)(2,1)} all-to-all(bf16[32,64,2880]{2,1,0:T(8,128)(2,1)} %bitcast.116), channel_id=1, replica_groups=mesh['dp'=4,'expert'=8] {'dp','expert'}, dimensions={0} | all-to-all | bytes 23592960 | tf_op jit(solution)/shard_map/all_to_all | solution.py:172
  466.6 15.1 %fusion.4 = f32[2048,720]{0,1:T(8,128)} fusion(bf16[2048,2880]{1,0:T(8,128)(2,1)} %bitcast.27, bf16[1,2880,720]{1,2,0:T(8,128)(2,1)} %param.34), kind=kOutput, calls=%fused_computation.15 | convolution fusion | flops 8493465600 | bytes 21841920 | tf_op jit(solution)/shard_map/dot_general | solution.py:177
  481.7 26.6 %convolution_convert_fusion = bf16[2048,2880]{0,1:T(8,128)(2,1)} fusion(bf16[1,720,2880]{2,1,0:T(8,128)(2,1)} %param.35, f32[2048,720]{0,1:T(8,128)} %fusion.4, bf16[2048,2880]{1,0:T(8,128)(2,1)} %bitcast.27, bf16[1,2880,720]{1,2,0:T(8,128)(2,1)} %param.33), kind=kOutput, calls=%fused_computation.4 | convolution fusion | flops 17004625920 | bytes 37785600 | tf_op jit(solution)/shard_map/dot_general | solution.py:182
  508.3 16.3 %copy.67 = bf16[2048,2880]{1,0:T(8,128)(2,1)} copy(bf16[2048,2880]{0,1:T(8,128)(2,1)} %convolution_convert_fusion) | data formatting | bytes 23592960 | tf_op jit(solution)/shard_map/convert_element_type | solution.py:183
  524.6 4.1 all-to-all-start.1
  529.4 266.6 %all-to-all-done.1 = bf16[32,64,2880]{2,1,0:T(8,128)(2,1)} async-done(((bf16[32,64,2880]{2,1,0:T(8,128)(2,1)}), bf16[32,64,2880]{2,1,0:T(8,128)(2,1)}, u32[]{:S(2)}, u32[]{:S(2)}) %all-to-all-start.1) | async-done | bytes 11796512 | tf_op jit(solution)/shard_map/all_to_all | solution.py:186
  796.0 6.8 reduce_sum.102
  802.9 3.5 gather_fusion.1
  806.3 2.6 gather.19
  808.9 4.7 multiply_reduce_fusion
  814.0 1.7 add_convert_fusion
  816.0 0.6 gather_fusion.2
  816.8 1.1 copy.68
  817.9 3.5 all-to-all-start.2
  821.5 49.2 %all-gather.1 = bf16[32,4,2880]{2,1,0:T(4,128)(2,1)} all-gather(bf16[1,4,2880]{2,1,0:T(4,128)(2,1)S(1)} %fusion.60), channel_id=1, replica_groups=mesh['dp'=4,'expert'=8] {'dp','expert'}, dimensions={0}, use_global_device_ids=true | all-gather | bytes 760320 | tf_op jit(solution)/shard_map/all_gather | solution.py:209
  870.7 2.3 reshape.444
  873.0 2.0 reduce_sum.104
  875.0 4.5 fusion.79
  879.4 1.0 copy.70
  (75 shorter events, 4.8 us)
Async XLA Ops:
  7.2 75.4 %copy-start = (bf16[512,2880]{0,1:T(8,128)(2,1)S(1)}, bf16[512,2880]{0,1:T(8,128)(2,1)}, u32[]{:S(2)}) copy-start(bf16[512,2880]{0,1:T(8,128)(2,1)} %param.27) | copy-start | bytes 8847364
  7.2 53.2 %all-gather.5.cloned.1.call-start = ((), (), s32[]{:S(2)}) async-start(), calls=%async_computation.4 | async-start | bytes 2764800 | tf_op jit(solution)/shard_map/all_gather | solution.py:101
  7.9 126.6 %reduce-scatter.2.cloned.1.call-start = ((), (), s32[]{:S(2)}) async-start(), calls=%async_computation.5 | async-start | bytes 2764800 | tf_op jit(solution)/shard_map/reduce_scatter | solution.py:133
  62.6 6.0 copy-start.8
  62.6 6.0 copy-start.9
  81.9 0.8 copy-start.3
  82.6 51.9 %copy-start.2 = (bf16[384,720]{0,1:T(8,128)(2,1)S(1)}, bf16[384,720]{0,1:T(8,128)(2,1)}, u32[]{:S(2)}) copy-start(bf16[384,720]{0,1:T(8,128)(2,1)} %param.19) | copy-start | bytes 1658884
  85.7 51.3 %copy-start.4 = (s32[1,96,4]{1,2,0:T(4,128)S(1)}, s32[1,96,4]{1,2,0:T(4,128)}, u32[]{:S(2)}) copy-start(s32[1,96,4]{1,2,0:T(4,128)} %param.22) | copy-start | bytes 4612
  85.7 101.7 %copy-start.5 = (f32[2880]{0:T(1024)S(1)}, f32[2880]{0:T(1024)}, u32[]{:S(2)}) copy-start(f32[2880]{0:T(1024)} %param.32) | copy-start | bytes 34564
  85.7 99.6 %all-gather.7.cloned.1.call-start = ((), (), s32[]{:S(2)}) async-start(), calls=%async_computation.6 | async-start | bytes 2764800 | tf_op jit(solution)/shard_map/all_gather | solution.py:151
  524.6 4.5 copy-start.7
  524.6 271.4 %all-to-all-start.1 = ((bf16[32,64,2880]{2,1,0:T(8,128)(2,1)}), bf16[32,64,2880]{2,1,0:T(8,128)(2,1)}, u32[]{:S(2)}, u32[]{:S(2)}) async-start(bf16[32,64,2880]{2,1,0:T(8,128)(2,1)} %bitcast.115), calls=%async_computation.2 | async-start | bytes 24117248 | tf_op jit(solution)/shard_map/all_to_all | solution.py:186
  813.6 7.8 copy-start.6
  817.9 61.5 %all-to-all-start.2 = ((bf16[96,4,720]{2,0,1:T(8,128)(2,1)}), bf16[96,4,720]{2,0,1:T(8,128)(2,1)S(1)}, u32[]{:S(2)}, u32[]{:S(2)}) async-start(bf16[96,4,720]{2,0,1:T(8,128)(2,1)} %copy.68), calls=%async_computation.3 | async-start | bytes 1179648 | tf_op jit(solution)/shard_map/all_to_all | solution.py:198
  821.5 59.0 %copy-start.1 = (bf16[512,2880]{0,1:T(8,128)(2,1)S(1)}, bf16[512,2880]{0,1:T(8,128)(2,1)}, u32[]{:S(2)}) copy-start(bf16[512,2880]{0,1:T(8,128)(2,1)} %param.27) | copy-start | bytes 8847364
Sparse Core Ops, SparseCore 0:
  9.6 50.7 all-gather.4
  85.8 48.6 reduce-scatter.1
  137.1 48.1 all-gather.6
